TPU v7x, 32 devices: a whole 2x2x4 slice. The times are simulated.
32 devices in a mesh: ctx: 8 (over z, y), seq: 4 (over x, core).
Axes of the slice: x: 2, y: 2, z: 4, core: 2. Of those that a mesh axis runs over, the one named last changes fastest.
Arguments:
- queries: bfloat16 [32768, 2048], P(('ctx', 'seq')), may hold values from -6 to 6
- keys: bfloat16 [32768, 2048], P(('ctx', 'seq')), may hold values from -6 to 6
- values: bfloat16 [32768, 2048], P(('ctx', 'seq')), may hold values from -6 to 6
- mixing: float32 [10, 16, 32768], P(None, None, ('ctx', 'seq')), may hold values from 0 to 1, as said below
Outputs:
- attended: float32 [32768, 2048], P(('ctx', 'seq'))
Inputs may be any that keep to these rules, and one draw needn't show every extreme that they name: Every mixing weight is positive and at most 1.
All inputs are finite; a program needn't handle non-finite values.
Results may differ from a plain program's by a relative error of at most 0.0028.
Values sent between devices are 32-bit elements; how exact they have to be, the bound alone decides.
No kernel may reach another device: no remote copies, remote signals or barrier semaphores. Data moves between devices by JAX's collectives and lax.ppermute only.
A program may use at most 192 MiB of HBM per device.

v0:
```python
import jax
import jax.numpy as jnp
from jax import lax
from jax.sharding import PartitionSpec as P

SPAN = 64


def partner_2(block, axis, bit):
    count = lax.axis_size(axis)
    route = []
    for low in range(count):
        high = low | 1 << bit
        if high != low and high < count:
            route += [(low, high), (high, low)]
    return lax.ppermute(block, axis, route)


def weighted_local(queries, keys, values, mixing, level_count):
    row_count = queries.shape[0]
    head_count = mixing.shape[1]
    key_width = queries.shape[1] // head_count
    value_width = values.shape[1] // head_count
    scale_factor = key_width ** (-0.5)
    positions = jnp.arange(row_count, dtype=jnp.int32)
    span_of = positions // SPAN
    crossed = jnp.bitwise_xor(span_of[:, None], span_of[None, :])
    level_map = jnp.zeros((row_count, row_count), jnp.int32)
    for power_index in range(level_count - 1):
        level_map = level_map + (crossed >= 2**power_index).astype(jnp.int32)
    causal = positions[:, None] >= positions[None, :]

    def one_head(head_index):
        query_head = lax.dynamic_slice_in_dim(queries, head_index * key_width, key_width, 1)
        key_head = lax.dynamic_slice_in_dim(keys, head_index * key_width, key_width, 1)
        value_head = lax.dynamic_slice_in_dim(values, head_index * value_width, value_width, 1)
        scores = jnp.dot(query_head, key_head.T, preferred_element_type=jnp.float32) * scale_factor
        head_mix = lax.dynamic_index_in_dim(mixing, head_index, 1, keepdims=False)
        weights = jnp.zeros_like(scores)
        for level_index in range(level_count):
            weights = weights + jnp.where(
                level_map == level_index, head_mix[level_index][:, None], 0.0
            )
        mixed_scores = jnp.where(causal, scores * weights, 0.0).astype(jnp.bfloat16)
        return jnp.dot(mixed_scores, value_head, preferred_element_type=jnp.float32)

    per_head = lax.map(one_head, jnp.arange(head_count, dtype=jnp.int32))
    return per_head.transpose(1, 0, 2).reshape(row_count, head_count * value_width)


def shards(queries, keys, values, mixing):
    row_count = queries.shape[0]
    head_count = mixing.shape[1]
    key_width = queries.shape[1] // head_count
    value_width = values.shape[1] // head_count
    scale_factor = key_width ** (-0.5)
    level_count = (row_count // SPAN).bit_length()
    local_out = weighted_local(queries, keys, values, mixing, level_count)
    query_head_rows = queries.reshape(row_count, head_count, key_width)
    own_state = jnp.einsum(
        "xej,xec->ejc",
        keys.reshape(row_count, head_count, key_width),
        values.reshape(row_count, head_count, value_width),
        preferred_element_type=jnp.float32,
    )
    seq_bits = lax.axis_size("seq").bit_length() - 1
    ctx_bits = lax.axis_size("ctx").bit_length() - 1
    seq_place = lax.axis_index("seq")
    ctx_place = lax.axis_index("ctx")
    sibling_sums = []
    flag_list = []
    running = own_state
    for bit_index in range(seq_bits):
        partner = partner_2(running, "seq", bit_index)
        sibling_sums.append(partner)
        flag_list.append(seq_place >> bit_index & 1)
        running = running + partner
    piece = lax.all_gather(running[None], "ctx", axis=0, tiled=True)
    owners = jnp.arange(piece.shape[0], dtype=jnp.int32)
    columns = []
    for add_bit_index in range(ctx_bits):
        same_high = owners >> add_bit_index + 1 == ctx_place >> add_bit_index + 1
        lower_half = owners >> add_bit_index & 1 == 0
        chosen = jnp.logical_and(same_high, lower_half)
        columns.append(jnp.sum(jnp.where(chosen[:, None, None, None], piece, 0.0), axis=0))
    gathered_blocks = jnp.stack(columns, axis=0)
    for bit_index in range(ctx_bits):
        sibling_sums.append(gathered_blocks[bit_index])
        flag_list.append(ctx_place >> bit_index & 1)
    cross = jnp.zeros((row_count, head_count, value_width), jnp.float32)
    for position in range(len(sibling_sums)):
        flag = flag_list[position].astype(jnp.float32)
        rounded_down = (flag * sibling_sums[position]).astype(jnp.bfloat16)
        level_mix = mixing[level_count + position].T
        weight_now = level_mix * scale_factor
        level_term = jnp.einsum(
            "cxm,xms->cxs", query_head_rows, rounded_down, preferred_element_type=jnp.float32
        )
        cross = cross + weight_now[:, :, None] * level_term
    return local_out + cross.reshape(row_count, head_count * value_width)


def solution(mesh):
    return jax.shard_map(
        shards,
        mesh=mesh,
        in_specs=(
            P(("ctx", "seq"), None),
            P(("ctx", "seq"), None),
            P(("ctx", "seq"), None),
            P(None, None, ("ctx", "seq")),
        ),
        out_specs=P(("ctx", "seq"), None),
        check_vma=False,
    )
```

profile of v0, /device:TPU:25, one launch (start us, length us, event | category | flops | bytes accessed | tf_op | source)
XLA Modules:
  0.0 240.6 jit_solution(2842181011538277074)
XLA Ops:
  6.5 6.4 %copy.35 = bf16[1024,2048]{0,1:T(8,128)(2,1)} copy(bf16[1024,2048]{1,0:T(8,128)(2,1)} %param.7) | data formatting | bytes 8388608 | tf_op jit(solution)/shard_map/reshape | solution.py:62
  12.9 4.8 %fusion.36 = f32[16,128,128]{2,1,0:T(8,128)S(1)} fusion(bf16[1024,16,128]{0,2,1:T(8,128)(2,1)} %bitcast.117, bf16[1024,2048]{1,0:T(8,128)(2,1)} %param.8), kind=kOutput, calls=%fused_computation.51 | convolution fusion | flops 536870912 | bytes 9437184 | tf_op jit(solution)/shard_map/xej,xec->ejc/dot_general | solution.py:60
  17.8 0.7 collective-permute-start
  18.5 2.3 collective-permute-done
  20.9 1.3 collective-permute-start.1
  22.2 1.0 multiply_bitcast_fusion.4
  23.2 22.1 %collective-permute-done.1 = f32[16,128,128]{2,1,0:T(8,128)S(1)} collective-permute-done((f32[16,128,128]{2,1,0:T(8,128)S(1)}, f32[16,128,128]{2,1,0:T(8,128)S(1)}, u32[]{:S(2)}, u32[]{:S(2)}) %collective-permute-start.1) | collective-permute-done | bytes 1048608 | tf_op jit(solution)/shard_map/ppermute | solution.py:16
  45.3 1.1 add.95
  46.4 133.1 %while.12 = (s32[]{:T(128)}, f32[16,1024,128]{1,2,0:T(8,128)}, s32[16]{0:T(128)S(1)}, bf16[1024,2048]{1,0:T(8,128)(2,1)}, bf16[1024,2048]{1,0:T(8,128)(2,1)}, /*...) while((s32[]{:T(128)}, f32[16,1024,128]{1,2,0:T(8,128)}, ...), condition=%wide.region_1.2_spmd.clone.clone, body=%wide.region_0.1_spmd.clone.clone.sunk | while | flops 569376768 | bytes 1382725 | solution.py:47
  48.7 0.9 constant_dynamic-slice_fusion.6
  50.1 4.7 %fusion.68 = f32[16,1024,128]{1,2,0:T(8,128)} fusion(f32[16,1024,128]{1,2,0:T(8,128)} %get-tuple-element.218, s32[]{:T(128)S(6)} %copy.70, s32[1024]{0:T(1024)S(1)} %get-tuple-element.241, f32[1024]{0:T(1024)S(1)} %bitcast.122, f32[1024]{0:T(1024)S(1)} %bitcast.119, f32[1024]{0:T(1024)S(1)} %bitcast.120, f32[1024]{0:T(1024)S(1)} %bitcast.121, ...), kind=kOutput, calls=%fused_computation.11.clone.1 | convolution fusion | flops 569376768 | bytes 1341440 | tf_op jit(solution)/shard_map/while/body/eval_jaxpr/dot_general | solution.py:45
  56.9 0.9 constant_dynamic-slice_fusion.6
  58.4 4.8 %fusion.68 = f32[16,1024,128]{1,2,0:T(8,128)} fusion(f32[16,1024,128]{1,2,0:T(8,128)} %get-tuple-element.218, s32[]{:T(128)S(6)} %copy.70, s32[1024]{0:T(1024)S(1)} %get-tuple-element.241, f32[1024]{0:T(1024)S(1)} %bitcast.122, f32[1024]{0:T(1024)S(1)} %bitcast.119, f32[1024]{0:T(1024)S(1)} %bitcast.120, f32[1024]{0:T(1024)S(1)} %bitcast.121, ...), kind=kOutput, calls=%fused_computation.11.clone.1 | convolution fusion | flops 569376768 | bytes 1341440 | tf_op jit(solution)/shard_map/while/body/eval_jaxpr/dot_general | solution.py:45
  65.4 0.9 constant_dynamic-slice_fusion.6
  66.8 4.7 %fusion.68 = f32[16,1024,128]{1,2,0:T(8,128)} fusion(f32[16,1024,128]{1,2,0:T(8,128)} %get-tuple-element.218, s32[]{:T(128)S(6)} %copy.70, s32[1024]{0:T(1024)S(1)} %get-tuple-element.241, f32[1024]{0:T(1024)S(1)} %bitcast.122, f32[1024]{0:T(1024)S(1)} %bitcast.119, f32[1024]{0:T(1024)S(1)} %bitcast.120, f32[1024]{0:T(1024)S(1)} %bitcast.121, ...), kind=kOutput, calls=%fused_computation.11.clone.1 | convolution fusion | flops 569376768 | bytes 1341440 | tf_op jit(solution)/shard_map/while/body/eval_jaxpr/dot_general | solution.py:45
  73.7 0.9 constant_dynamic-slice_fusion.6
  75.1 4.7 %fusion.68 = f32[16,1024,128]{1,2,0:T(8,128)} fusion(f32[16,1024,128]{1,2,0:T(8,128)} %get-tuple-element.218, s32[]{:T(128)S(6)} %copy.70, s32[1024]{0:T(1024)S(1)} %get-tuple-element.241, f32[1024]{0:T(1024)S(1)} %bitcast.122, f32[1024]{0:T(1024)S(1)} %bitcast.119, f32[1024]{0:T(1024)S(1)} %bitcast.120, f32[1024]{0:T(1024)S(1)} %bitcast.121, ...), kind=kOutput, calls=%fused_computation.11.clone.1 | convolution fusion | flops 569376768 | bytes 1341440 | tf_op jit(solution)/shard_map/while/body/eval_jaxpr/dot_general | solution.py:45
  82.0 0.9 constant_dynamic-slice_fusion.6
  83.4 4.7 %fusion.68 = f32[16,1024,128]{1,2,0:T(8,128)} fusion(f32[16,1024,128]{1,2,0:T(8,128)} %get-tuple-element.218, s32[]{:T(128)S(6)} %copy.70, s32[1024]{0:T(1024)S(1)} %get-tuple-element.241, f32[1024]{0:T(1024)S(1)} %bitcast.122, f32[1024]{0:T(1024)S(1)} %bitcast.119, f32[1024]{0:T(1024)S(1)} %bitcast.120, f32[1024]{0:T(1024)S(1)} %bitcast.121, ...), kind=kOutput, calls=%fused_computation.11.clone.1 | convolution fusion | flops 569376768 | bytes 1341440 | tf_op jit(solution)/shard_map/while/body/eval_jaxpr/dot_general | solution.py:45
  90.3 0.9 constant_dynamic-slice_fusion.6
  91.7 4.7 %fusion.68 = f32[16,1024,128]{1,2,0:T(8,128)} fusion(f32[16,1024,128]{1,2,0:T(8,128)} %get-tuple-element.218, s32[]{:T(128)S(6)} %copy.70, s32[1024]{0:T(1024)S(1)} %get-tuple-element.241, f32[1024]{0:T(1024)S(1)} %bitcast.122, f32[1024]{0:T(1024)S(1)} %bitcast.119, f32[1024]{0:T(1024)S(1)} %bitcast.120, f32[1024]{0:T(1024)S(1)} %bitcast.121, ...), kind=kOutput, calls=%fused_computation.11.clone.1 | convolution fusion | flops 569376768 | bytes 1341440 | tf_op jit(solution)/shard_map/while/body/eval_jaxpr/dot_general | solution.py:45
  98.6 0.9 constant_dynamic-slice_fusion.6
  100.0 4.9 %fusion.68 = f32[16,1024,128]{1,2,0:T(8,128)} fusion(f32[16,1024,128]{1,2,0:T(8,128)} %get-tuple-element.218, s32[]{:T(128)S(6)} %copy.70, s32[1024]{0:T(1024)S(1)} %get-tuple-element.241, f32[1024]{0:T(1024)S(1)} %bitcast.122, f32[1024]{0:T(1024)S(1)} %bitcast.119, f32[1024]{0:T(1024)S(1)} %bitcast.120, f32[1024]{0:T(1024)S(1)} %bitcast.121, ...), kind=kOutput, calls=%fused_computation.11.clone.1 | convolution fusion | flops 569376768 | bytes 1341440 | tf_op jit(solution)/shard_map/while/body/eval_jaxpr/dot_general | solution.py:45
  107.1 0.9 constant_dynamic-slice_fusion.6
  108.5 4.7 %fusion.68 = f32[16,1024,128]{1,2,0:T(8,128)} fusion(f32[16,1024,128]{1,2,0:T(8,128)} %get-tuple-element.218, s32[]{:T(128)S(6)} %copy.70, s32[1024]{0:T(1024)S(1)} %get-tuple-element.241, f32[1024]{0:T(1024)S(1)} %bitcast.122, f32[1024]{0:T(1024)S(1)} %bitcast.119, f32[1024]{0:T(1024)S(1)} %bitcast.120, f32[1024]{0:T(1024)S(1)} %bitcast.121, ...), kind=kOutput, calls=%fused_computation.11.clone.1 | convolution fusion | flops 569376768 | bytes 1341440 | tf_op jit(solution)/shard_map/while/body/eval_jaxpr/dot_general | solution.py:45
  115.4 0.9 constant_dynamic-slice_fusion.6
  116.8 4.7 %fusion.68 = f32[16,1024,128]{1,2,0:T(8,128)} fusion(f32[16,1024,128]{1,2,0:T(8,128)} %get-tuple-element.218, s32[]{:T(128)S(6)} %copy.70, s32[1024]{0:T(1024)S(1)} %get-tuple-element.241, f32[1024]{0:T(1024)S(1)} %bitcast.122, f32[1024]{0:T(1024)S(1)} %bitcast.119, f32[1024]{0:T(1024)S(1)} %bitcast.120, f32[1024]{0:T(1024)S(1)} %bitcast.121, ...), kind=kOutput, calls=%fused_computation.11.clone.1 | convolution fusion | flops 569376768 | bytes 1341440 | tf_op jit(solution)/shard_map/while/body/eval_jaxpr/dot_general | solution.py:45
  123.7 0.9 constant_dynamic-slice_fusion.6
  125.1 4.7 %fusion.68 = f32[16,1024,128]{1,2,0:T(8,128)} fusion(f32[16,1024,128]{1,2,0:T(8,128)} %get-tuple-element.218, s32[]{:T(128)S(6)} %copy.70, s32[1024]{0:T(1024)S(1)} %get-tuple-element.241, f32[1024]{0:T(1024)S(1)} %bitcast.122, f32[1024]{0:T(1024)S(1)} %bitcast.119, f32[1024]{0:T(1024)S(1)} %bitcast.120, f32[1024]{0:T(1024)S(1)} %bitcast.121, ...), kind=kOutput, calls=%fused_computation.11.clone.1 | convolution fusion | flops 569376768 | bytes 1341440 | tf_op jit(solution)/shard_map/while/body/eval_jaxpr/dot_general | solution.py:45
  132.0 0.9 constant_dynamic-slice_fusion.6
  133.4 4.7 %fusion.68 = f32[16,1024,128]{1,2,0:T(8,128)} fusion(f32[16,1024,128]{1,2,0:T(8,128)} %get-tuple-element.218, s32[]{:T(128)S(6)} %copy.70, s32[1024]{0:T(1024)S(1)} %get-tuple-element.241, f32[1024]{0:T(1024)S(1)} %bitcast.122, f32[1024]{0:T(1024)S(1)} %bitcast.119, f32[1024]{0:T(1024)S(1)} %bitcast.120, f32[1024]{0:T(1024)S(1)} %bitcast.121, ...), kind=kOutput, calls=%fused_computation.11.clone.1 | convolution fusion | flops 569376768 | bytes 1341440 | tf_op jit(solution)/shard_map/while/body/eval_jaxpr/dot_general | solution.py:45
  140.3 0.9 constant_dynamic-slice_fusion.6
  141.7 4.7 %fusion.68 = f32[16,1024,128]{1,2,0:T(8,128)} fusion(f32[16,1024,128]{1,2,0:T(8,128)} %get-tuple-element.218, s32[]{:T(128)S(6)} %copy.70, s32[1024]{0:T(1024)S(1)} %get-tuple-element.241, f32[1024]{0:T(1024)S(1)} %bitcast.122, f32[1024]{0:T(1024)S(1)} %bitcast.119, f32[1024]{0:T(1024)S(1)} %bitcast.120, f32[1024]{0:T(1024)S(1)} %bitcast.121, ...), kind=kOutput, calls=%fused_computation.11.clone.1 | convolution fusion | flops 569376768 | bytes 1341440 | tf_op jit(solution)/shard_map/while/body/eval_jaxpr/dot_general | solution.py:45
  148.6 0.9 constant_dynamic-slice_fusion.6
  150.0 4.7 %fusion.68 = f32[16,1024,128]{1,2,0:T(8,128)} fusion(f32[16,1024,128]{1,2,0:T(8,128)} %get-tuple-element.218, s32[]{:T(128)S(6)} %copy.70, s32[1024]{0:T(1024)S(1)} %get-tuple-element.241, f32[1024]{0:T(1024)S(1)} %bitcast.122, f32[1024]{0:T(1024)S(1)} %bitcast.119, f32[1024]{0:T(1024)S(1)} %bitcast.120, f32[1024]{0:T(1024)S(1)} %bitcast.121, ...), kind=kOutput, calls=%fused_computation.11.clone.1 | convolution fusion | flops 569376768 | bytes 1341440 | tf_op jit(solution)/shard_map/while/body/eval_jaxpr/dot_general | solution.py:45
  156.9 0.9 constant_dynamic-slice_fusion.6
  158.3 4.7 %fusion.68 = f32[16,1024,128]{1,2,0:T(8,128)} fusion(f32[16,1024,128]{1,2,0:T(8,128)} %get-tuple-element.218, s32[]{:T(128)S(6)} %copy.70, s32[1024]{0:T(1024)S(1)} %get-tuple-element.241, f32[1024]{0:T(1024)S(1)} %bitcast.122, f32[1024]{0:T(1024)S(1)} %bitcast.119, f32[1024]{0:T(1024)S(1)} %bitcast.120, f32[1024]{0:T(1024)S(1)} %bitcast.121, ...), kind=kOutput, calls=%fused_computation.11.clone.1 | convolution fusion | flops 569376768 | bytes 1341440 | tf_op jit(solution)/shard_map/while/body/eval_jaxpr/dot_general | solution.py:45
  165.1 0.9 constant_dynamic-slice_fusion.6
  166.6 4.7 %fusion.68 = f32[16,1024,128]{1,2,0:T(8,128)} fusion(f32[16,1024,128]{1,2,0:T(8,128)} %get-tuple-element.218, s32[]{:T(128)S(6)} %copy.70, s32[1024]{0:T(1024)S(1)} %get-tuple-element.241, f32[1024]{0:T(1024)S(1)} %bitcast.122, f32[1024]{0:T(1024)S(1)} %bitcast.119, f32[1024]{0:T(1024)S(1)} %bitcast.120, f32[1024]{0:T(1024)S(1)} %bitcast.121, ...), kind=kOutput, calls=%fused_computation.11.clone.1 | convolution fusion | flops 569376768 | bytes 1341440 | tf_op jit(solution)/shard_map/while/body/eval_jaxpr/dot_general | solution.py:45
  173.4 0.9 constant_dynamic-slice_fusion.6
  174.8 4.7 %fusion.68 = f32[16,1024,128]{1,2,0:T(8,128)} fusion(f32[16,1024,128]{1,2,0:T(8,128)} %get-tuple-element.218, s32[]{:T(128)S(6)} %copy.70, s32[1024]{0:T(1024)S(1)} %get-tuple-element.241, f32[1024]{0:T(1024)S(1)} %bitcast.122, f32[1024]{0:T(1024)S(1)} %bitcast.119, f32[1024]{0:T(1024)S(1)} %bitcast.120, f32[1024]{0:T(1024)S(1)} %bitcast.121, ...), kind=kOutput, calls=%fused_computation.11.clone.1 | convolution fusion | flops 569376768 | bytes 1341440 | tf_op jit(solution)/shard_map/while/body/eval_jaxpr/dot_general | solution.py:45
  179.5 6.8 %fusion.34 = f32[16,128,1024]{2,1,0:T(8,128)} fusion(f32[16,128,128]{2,1,0:T(8,128)S(1)} %collective-permute-done, f32[]{:T(128)S(6)} %convert_element_type.81, bf16[1024,2048]{1,0:T(8,128)(2,1)} %get-tuple-element.252), kind=kOutput, calls=%fused_computation.49 | convolution fusion | flops 537395200 | bytes 13631492 | tf_op jit(solution)/shard_map/cxm,xms->cxs/dot_general | solution.py:96
  186.3 5.0 %select_reduce_fusion.2 = (f32[16,128,128]{2,1,0:T(8,128)S(1)}, f32[16,128,128]{2,1,0:T(8,128)S(1)}, f32[16,128,128]{2,1,0:T(8,128)S(1)}) fusion(f32[8,16,128,128]{3,2,1,0:T(8,128)} %bitcast.116, pred[8]{0:T(512)(128)(4,1)S(1)} %compare_and_fusion.2, pred[8]{0:T(512)(128)(4,1)S(1)} %get-tuple-element.139, pred[8]{0:T(512)(128)(4,1)S(1)} %get-tuple-element.140), kind=kLoop, calls=%fused_computation.40 | loop fusion | flops 11796480 | bytes 11534360 | tf_op jit(solution)/shard_map/reduce_sum | solution.py:85
  191.3 4.6 %fusion.26 = f32[16,128,1024]{2,1,0:T(8,128)} fusion(f32[16,128,128]{2,1,0:T(8,128)S(1)} %get-tuple-element.111, f32[]{:T(128)S(6)} %convert_element_type.89, bf16[1024,2048]{1,0:T(8,128)(2,1)S(1)} %copy-done), kind=kOutput, calls=%fused_computation.41 | convolution fusion | flops 537395200 | bytes 13631492 | tf_op jit(solution)/shard_map/cxm,xms->cxs/dot_general | solution.py:96
  195.9 4.6 %fusion.28 = f32[16,128,1024]{2,1,0:T(8,128)} fusion(f32[16,128,128]{2,1,0:T(8,128)S(1)} %get-tuple-element.112, f32[]{:T(128)S(6)} %convert_element_type.87, bf16[1024,2048]{1,0:T(8,128)(2,1)S(1)} %copy-done), kind=kOutput, calls=%fused_computation.43 | convolution fusion | flops 537395200 | bytes 13631492 | tf_op jit(solution)/shard_map/cxm,xms->cxs/dot_general | solution.py:96
  200.5 4.6 %fusion.30 = f32[16,128,1024]{2,1,0:T(8,128)} fusion(f32[16,128,128]{2,1,0:T(8,128)S(1)} %get-tuple-element.110, f32[]{:T(128)S(6)} %convert_element_type.85, bf16[1024,2048]{1,0:T(8,128)(2,1)S(1)} %copy-done), kind=kOutput, calls=%fused_computation.45 | convolution fusion | flops 537395200 | bytes 13631492 | tf_op jit(solution)/shard_map/cxm,xms->cxs/dot_general | solution.py:96
  205.1 19.6 %fusion.22 = f32[1024,16,128]{0,2,1:T(8,128)} fusion(f32[16,128,1024]{2,1,0:T(8,128)} %fusion.26, f32[16,128,1024]{2,1,0:T(8,128)} %fusion.28, f32[16,128,1024]{2,1,0:T(8,128)} %fusion.30, f32[16,128,1024]{2,1,0:T(8,128)} %fusion.34, f32[16,1024,128]{1,2,0:T(8,128)} %get-tuple-element.64, f32[1024,16]{0,1:T(8,128)S(1)} %get-tuple-element.137, ...), kind=kOutput, calls=%fused_computation.30 | convolution fusion | flops 558366720 | bytes 55902212 | tf_op jit(solution)/shard_map/cxm,xms->cxs/dot_general | solution.py:96
  224.6 9.1 %copy.29 = f32[1024,2048]{1,0:T(8,128)} copy(f32[1024,2048]{0,1:T(8,128)} %bitcast.115) | data formatting | bytes 16777216 | tf_op jit(solution)/shard_map/add | solution.py:100
  (27 shorter events, 8.9 us)
Async XLA Ops:
  6.5 179.8 %all-gather.3.cloned.1.call-start = ((), (), s32[]{:S(2)}) async-start(), calls=%async_computation | async-start | bytes 9437184 | tf_op jit(solution)/shard_map/all_gather | solution.py:78
  17.8 3.0 %collective-permute-start = (f32[16,128,128]{2,1,0:T(8,128)S(1)}, f32[16,128,128]{2,1,0:T(8,128)S(1)}, u32[]{:S(2)}, u32[]{:S(2)}) collective-permute-start(f32[16,128,128]{2,1,0:T(8,128)S(1)} %fusion.36), channel_id=1, source_target_pairs={{0,1},{1,0},{2,3},{3,2},{4,5},{5,4},{6,7},{7,6},{8,9},{9,8},{10,11... | collective-permute-start | bytes 3145736 | tf_op jit(solution)/shard_map/ppermute | solution.py:16
  20.9 24.4 %collective-permute-start.1 = (f32[16,128,128]{2,1,0:T(8,128)S(1)}, f32[16,128,128]{2,1,0:T(8,128)S(1)}, u32[]{:S(2)}, u32[]{:S(2)}) collective-permute-start(f32[16,128,128]{2,1,0:T(8,128)S(1)} %add.93), channel_id=1, source_target_pairs={{0,2},{2,0},{1,3},{3,1},{4,6},{6,4},{5,7},{7,5},{8,10},{10,8},{9,1... | collective-permute-start | bytes 3145736 | tf_op jit(solution)/shard_map/ppermute | solution.py:16
  186.3 5.0 %copy-start = (bf16[1024,2048]{1,0:T(8,128)(2,1)S(1)}, bf16[1024,2048]{1,0:T(8,128)(2,1)}, u32[]{:S(2)}) copy-start(bf16[1024,2048]{1,0:T(8,128)(2,1)} %get-tuple-element.252) | copy-start | bytes 12582916
Sparse Core Ops, SparseCore 0:
  46.6 124.1 all-gather.2
where the time goes:
time: 245 us; the launch traced here: 241 us
  matrix products  120 us (49%)
  local copies, waits for them, and re-layouts  38 us (16%)
  loops' own time  35.1 us (14%)
  waiting for transfers between devices  24.4 us (10%)
  between operations  13.4 us (5%)
  other arithmetic  7.19 us (3%)
    dot_general x16, matrix products, one_head(): return jnp.dot(mixed_scores, value_head, preferred_element_type=jnp.float32)  75.5 us
    dot_general x5, matrix products, shards(): jnp.einsum('cxm,xms->cxs', query_head_rows, rounded_down, preferred_eleme...  40.1 us
    another operation x1, loops' own time, weighted_local(): per_head = lax.map(one_head, jnp.arange(head_count, dtype=jnp.int32))  35.1 us
    ppermute x2, waiting for transfers between devices, partner_2(): return lax.ppermute(block, axis, route)  24.4 us
    slice x16, local copies, waits for them, and re-layouts, one_head(): head_mix[level_index][:, None]  13.7 us
    add x1, local copies, waits for them, and re-layouts, shards(): return local_out + cross.reshape(row_count, head_count * value_width)  9.12 us
    dynamic_slice x16, local copies, waits for them, and re-layouts, weighted_local(): per_head = lax.map(one_head, jnp.arange(head_count, dtype=jnp.int32))  8.79 us
    reshape x1, local copies, waits for them, and re-layouts, shards(): keys.reshape(row_count, head_count, key_width)  6.39 us
  transfers between devices with their start and end apart: 3, of which 2 were waited for; matrix products, arithmetic and copies ran while one was open for 44% of the time, Pallas kernels for 0%

commit v1 on v0

v1 whole, which is shorter than its diff:
```python
import functools

import numpy as np
import jax
import jax.numpy as jnp
from jax import lax
from jax.experimental import pallas as pl
from jax.experimental.pallas import tpu as pltpu
from jax.sharding import PartitionSpec as P

SPAN = 64
TQ = 256
CHUNKS = 4


def level_masks(block, level_count):
    pos = np.arange(block)
    span = pos // SPAN
    crossed = span[:, None] ^ span[None, :]
    level = np.zeros_like(crossed)
    for power_index in range(level_count - 1):
        level = level + (crossed >= 2**power_index)
    causal = pos[:, None] >= pos[None, :]
    inner = int(np.log2(block // SPAN)) + 1
    return np.stack(
        [((level == l) & causal).astype(np.float32) for l in range(inner)]
    )


def state_kernel(k_ref, v_ref, o_ref):
    o_ref[0] = lax.dot_general(
        k_ref[...], v_ref[...], (((0,), (0,)), ((), ())),
        preferred_element_type=jnp.float32,
    )


def own_state(keys, values, head_count):
    rows, width = keys.shape
    dk = width // head_count
    dv = values.shape[1] // head_count
    return pl.pallas_call(
        state_kernel,
        grid=(head_count,),
        in_specs=[
            pl.BlockSpec((rows, dk), lambda h: (0, h)),
            pl.BlockSpec((rows, dv), lambda h: (0, h)),
        ],
        out_specs=pl.BlockSpec((1, dk, dv), lambda h: (h, 0, 0)),
        out_shape=jax.ShapeDtypeStruct((head_count, dk, dv), jnp.float32),
        cost_estimate=pl.CostEstimate(
            flops=2 * rows * dk * dv * head_count,
            bytes_accessed=2 * rows * (dk + dv) * head_count + 4 * dk * dv * head_count,
            transcendentals=0,
        ),
    )(keys, values)


def local_kernel(scale, rows, q_ref, k_ref, v_ref, m_ref, c_ref, o_ref):
    blocks = rows // TQ
    inner = c_ref.shape[0]
    for a in range(blocks):
        r0 = a * TQ
        qb = q_ref[r0:r0 + TQ, :]
        kk = k_ref[0:r0 + TQ, :]
        s = lax.dot_general(
            qb, kk, (((1,), (1,)), ((), ())), preferred_element_type=jnp.float32
        )
        s = s * scale
        mix = m_ref[0, r0:r0 + TQ, :]
        pieces = []
        for b in range(a):
            level = inner + (a ^ b).bit_length() - 1
            w = mix[:, level:level + 1]
            pieces.append((s[:, b * TQ:(b + 1) * TQ] * w).astype(jnp.bfloat16))
        wd = c_ref[0] * mix[:, 0:1]
        for l in range(1, inner):
            wd = wd + c_ref[l] * mix[:, l:l + 1]
        pieces.append((s[:, r0:r0 + TQ] * wd).astype(jnp.bfloat16))
        p = pieces[0] if len(pieces) == 1 else jnp.concatenate(pieces, axis=1)
        o_ref[r0:r0 + TQ, :] = jnp.dot(
            p, v_ref[0:r0 + TQ, :], preferred_element_type=jnp.float32
        )


def local_part(queries, keys, values, mix_t, masks, first, count, scale):
    rows = queries.shape[0]
    head_count = mix_t.shape[0]
    dk = queries.shape[1] // head_count
    dv = values.shape[1] // head_count
    levels = mix_t.shape[2]
    blocks = rows // TQ
    tiles = blocks * (blocks + 1) // 2
    return pl.pallas_call(
        functools.partial(local_kernel, scale, rows),
        grid=(count,),
        in_specs=[
            pl.BlockSpec((rows, dk), lambda h: (0, h + first)),
            pl.BlockSpec((rows, dk), lambda h: (0, h + first)),
            pl.BlockSpec((rows, dv), lambda h: (0, h + first)),
            pl.BlockSpec((1, rows, levels), lambda h: (h + first, 0, 0)),
            pl.BlockSpec(masks.shape, lambda h: (0, 0, 0)),
        ],
        out_specs=pl.BlockSpec((rows, dv), lambda h: (0, h)),
        out_shape=jax.ShapeDtypeStruct((rows, dv * count), jnp.float32),
        cost_estimate=pl.CostEstimate(
            flops=2 * tiles * TQ * TQ * (dk + dv) * count,
            bytes_accessed=(2 * rows * (2 * dk + dv) + 4 * rows * dv) * count,
            transcendentals=0,
        ),
        compiler_params=pltpu.CompilerParams(vmem_limit_bytes=64 * 1024 * 1024),
    )(queries, keys, values, mix_t, masks)


def cross_kernel(scale, rows, first_level, q_ref, s_ref, m_ref, l_ref, *rest):
    o_ref = rest[-1]
    bits = s_ref.shape[0]
    sib = jnp.concatenate([s_ref[b, 0] for b in range(bits)], axis=1)
    dv = s_ref.shape[3]
    for a in range(rows // TQ):
        r0 = a * TQ
        t = jnp.dot(q_ref[r0:r0 + TQ, :], sib, preferred_element_type=jnp.float32)
        mix = m_ref[0, r0:r0 + TQ, :]
        cross = jnp.zeros((TQ, dv), jnp.float32)
        for b in range(bits):
            w = mix[:, first_level + b:first_level + b + 1] * scale
            cross = cross + w * t[:, b * dv:(b + 1) * dv]
        o_ref[r0:r0 + TQ, :] = l_ref[r0:r0 + TQ, :] + cross


def cross_part(queries, sibs, mix_t, local, first, count, scale, first_level, prev):
    rows = queries.shape[0]
    head_count = mix_t.shape[0]
    dk = queries.shape[1] // head_count
    dv = sibs.shape[3]
    levels = mix_t.shape[2]
    bits = sibs.shape[0]
    in_specs = [
        pl.BlockSpec((rows, dk), lambda h: (0, h + first)),
        pl.BlockSpec((bits, 1, dk, dv), lambda h: (0, h + first, 0, 0)),
        pl.BlockSpec((1, rows, levels), lambda h: (h + first, 0, 0)),
        pl.BlockSpec((rows, dv), lambda h: (0, h)),
    ]
    operands = [queries, sibs, mix_t, local]
    aliases = {}
    if prev is not None:
        in_specs.append(pl.BlockSpec(memory_space=pl.ANY))
        operands.append(prev)
        aliases = {4: 0}
    return pl.pallas_call(
        functools.partial(cross_kernel, scale, rows, first_level),
        grid=(count,),
        in_specs=in_specs,
        out_specs=pl.BlockSpec((rows, dv), lambda h: (0, h + first)),
        out_shape=jax.ShapeDtypeStruct((rows, dv * head_count), jnp.float32),
        input_output_aliases=aliases,
        cost_estimate=pl.CostEstimate(
            flops=2 * rows * dk * dv * bits * count,
            bytes_accessed=(2 * rows * dk + 8 * rows * dv) * count,
            transcendentals=0,
        ),
        compiler_params=pltpu.CompilerParams(vmem_limit_bytes=64 * 1024 * 1024),
    )(*operands)


def swap(block, axis, bit, one_way=False):
    count = lax.axis_size(axis)
    route = []
    for low in range(count):
        high = low | 1 << bit
        if high != low and high < count:
            route.append((low, high))
            if not one_way:
                route.append((high, low))
    return lax.ppermute(block, axis, route)


def to_offset(block, axis, offset):
    count = lax.axis_size(axis)
    return lax.ppermute(block, axis, [(s, s ^ offset) for s in range(count)])


def shards(queries, keys, values, mixing):
    rows = queries.shape[0]
    head_count = mixing.shape[1]
    dk = queries.shape[1] // head_count
    scale = dk ** (-0.5)
    level_count = (rows // SPAN).bit_length()
    mix_t = mixing.transpose(1, 2, 0)
    masks = jnp.asarray(level_masks(TQ, level_count))

    state = own_state(keys, values, head_count)

    seq_count = lax.axis_size("seq")
    ctx_count = lax.axis_size("ctx")
    seq_bits = seq_count.bit_length() - 1
    ctx_bits = ctx_count.bit_length() - 1
    seq_place = lax.axis_index("seq")
    ctx_place = lax.axis_index("ctx")

    sibs = []
    flags = []
    running = state
    half = head_count // 2
    for bit in range(seq_bits):
        if bit == 0 or seq_count < 4:
            partner = swap(running, "seq", bit)
        else:
            mine = seq_place & 1
            sent = lax.dynamic_slice_in_dim(running, mine * half, half, 0)
            got = swap(sent, "seq", bit)
            other = swap(got, "seq", 0)
            lo = jnp.where(mine == 0, got, other)
            hi = jnp.where(mine == 0, other, got)
            partner = jnp.concatenate([lo, hi], axis=0)
        sibs.append(partner)
        flags.append(seq_place >> bit & 1)
        running = running + partner

    share = head_count // seq_count
    quarter = lax.dynamic_slice_in_dim(running, seq_place * share, share, 0)
    ctx_sibs = []
    for bit in range(ctx_bits):
        got = swap(quarter, "ctx", bit, one_way=(bit == ctx_bits - 1))
        ctx_sibs.append(got)
        if bit != ctx_bits - 1:
            quarter = quarter + got

    for bit in range(ctx_bits):
        part = ctx_sibs[bit]
        parts = {0: part}
        for offset in range(1, seq_count):
            if offset & 1 and offset > 1:
                parts[offset] = to_offset(parts[offset ^ 1], "seq", 1)
            else:
                parts[offset] = to_offset(part, "seq", offset)
        full = []
        for owner in range(seq_count):
            pick = jnp.zeros_like(part)
            for offset in range(seq_count):
                pick = jnp.where((seq_place ^ offset) == owner, parts[offset], pick)
            full.append(pick)
        sibs.append(jnp.concatenate(full, axis=0))
        flags.append(ctx_place >> bit & 1)

    rounded = jnp.stack(
        [(flags[i].astype(jnp.float32) * sibs[i]).astype(jnp.bfloat16) for i in range(len(sibs))]
    )

    per = head_count // CHUNKS
    out = None
    for c in range(CHUNKS):
        local = local_part(queries, keys, values, mix_t, masks, c * per, per, scale)
        out = cross_part(queries, rounded, mix_t, local, c * per, per, scale, level_count, out)
    return out


def solution(mesh):
    return jax.shard_map(
        shards,
        mesh=mesh,
        in_specs=(
            P(("ctx", "seq"), None),
            P(("ctx", "seq"), None),
            P(("ctx", "seq"), None),
            P(None, None, ("ctx", "seq")),
        ),
        out_specs=P(("ctx", "seq"), None),
        check_vma=False,
    )
```

time: 245 us -> 156 us (0.64); the launches traced: 241 us -> 154 us
  matrix products: 120 us -> 0 us
  Pallas kernels: 0 us -> 66.9 us
  loops' own time: 35.1 us -> 0 us
  local copies, waits for them, and re-layouts: 38 us -> 6.5 us
  waiting for transfers between devices: 24.4 us -> 52.2 us
  starting transfers between devices: 2.02 us -> 16.1 us
  between operations: 13.4 us -> 0.2 us
  other arithmetic: 7.19 us -> 12.4 us
    dot_general x22 -> x0, matrix products: 120 us -> none  [the longest x16 75.5 us: one_head(): return jnp.dot(mixed_scores, value_head, preferred_element_type=jnp.float32)]
    pallas_call x0 -> x9, Pallas kernels: none -> 66.9 us  [the longest x4 29.6 us: local_part(): pl.pallas_call(functools.partial(local_kernel, scale, rows), grid=(count,...]
    another operation x1 -> x0, loops' own time: 35.1 us -> none  [weighted_local(): per_head = lax.map(one_head, jnp.arange(head_count, dtype=jnp.int32))]
    ppermute x2 -> x15, waiting for transfers between devices: 24.4 us -> 52.2 us  [the longest x6 41.9 us: swap(): return lax.ppermute(block, axis, route)]
    ppermute x2 -> x15, starting transfers between devices: 2.02 us -> 16.1 us  [the longest x9 10 us: to_offset(): return lax.ppermute(block, axis, [(s, s ^ offset) for s in range(count)])]
    slice x16 -> x0, local copies, waits for them, and re-layouts: 13.7 us -> none  [one_head(): head_mix[level_index][:, None]]
    add x1 -> x0, local copies, waits for them, and re-layouts: 9.12 us -> none  [shards(): return local_out + cross.reshape(row_count, head_count * value_width)]
    dynamic_slice x16 -> x1, local copies, waits for them, and re-layouts: 8.79 us -> 0.04 us  [shards(): sent = lax.dynamic_slice_in_dim(running, mine * half, half, 0)]
  transfers between devices with their start and end apart: 3 -> 15, of which waited for: 2 -> 9; matrix products, arithmetic and copies ran while one was open for 44% -> 7% of each run, Pallas kernels for 0% -> 19%
where the time goes in v1:
time: 156 us; the launch traced here: 154 us
  Pallas kernels  66.9 us (43%)
  waiting for transfers between devices  52.2 us (33%)
  starting transfers between devices  16.1 us (10%)
  other arithmetic  12.4 us (8%)
  local copies, waits for them, and re-layouts  6.5 us (4%)
    ppermute x6, waiting for transfers between devices, swap(): return lax.ppermute(block, axis, route)  41.9 us
    pallas_call x4, Pallas kernels, local_part(): pl.pallas_call(functools.partial(local_kernel, scale, rows), grid=(count,...  29.6 us
    pallas_call x4, Pallas kernels, cross_part(): pl.pallas_call(functools.partial(cross_kernel, scale, rows, first_level),...  25.2 us
    pallas_call x1, Pallas kernels, own_state(): pl.pallas_call(state_kernel, grid=(head_count,), in_specs=[pl.BlockSpec((...  12.2 us
    ppermute x9, waiting for transfers between devices, to_offset(): return lax.ppermute(block, axis, [(s, s ^ offset) for s in range(count)])  10.3 us
    ppermute x9, starting transfers between devices, to_offset(): return lax.ppermute(block, axis, [(s, s ^ offset) for s in range(count)])  10 us
    unnamed x33, local copies, waits for them, and re-layouts  6.46 us
    ppermute x6, starting transfers between devices, swap(): return lax.ppermute(block, axis, route)  6.02 us
  transfers between devices with their start and end apart: 15, of which 9 were waited for; matrix products, arithmetic and copies ran while one was open for 7% of the time, Pallas kernels for 19%

profile of v1, /device:TPU:25, one launch (start us, length us, event | category | flops | bytes accessed | tf_op | source)
XLA Modules:
  0.0 154.3 jit_solution(2528565216941826220)
XLA Ops:
  0.0 12.2 %shard_map.55 = f32[16,128,128]{2,1,0:T(8,128)} custom-call(bf16[1024,2048]{1,0:T(8,128)(2,1)} %k_ref.9, bf16[1024,2048]{1,0:T(8,128)(2,1)} %v_ref.9), custom_call_target="tpu_custom_call" | custom-call | flops 536870912 | bytes 9437184 | tf_op jit(solution)/shard_map/pallas_call | solution.py:41
  12.2 0.7 collective-permute-start
  12.8 2.5 %collective-permute-done = f32[16,128,128]{2,1,0:T(8,128)S(1)} collective-permute-done((f32[16,128,128]{2,1,0:T(8,128)}, f32[16,128,128]{2,1,0:T(8,128)S(1)}, u32[]{:S(2)}, u32[]{:S(2)}) %collective-permute-start) | collective-permute-done | bytes 1048608 | tf_op jit(solution)/shard_map/ppermute | solution.py:174
  15.3 1.7 %add.18 = f32[16,128,128]{2,1,0:T(8,128)S(1)} add(f32[16,128,128]{2,1,0:T(8,128)} %shard_map.55, f32[16,128,128]{2,1,0:T(8,128)S(1)} %collective-permute-done) | non-fusion elementwise | flops 262144 | bytes 3145728 | tf_op jit(solution)/shard_map/add | solution.py:217
  17.1 1.3 collective-permute-start.1
  18.4 11.9 %collective-permute-done.1 = f32[8,128,128]{2,1,0:T(8,128)S(1)} collective-permute-done((f32[8,128,128]{2,1,0:T(8,128)S(1)}, f32[8,128,128]{2,1,0:T(8,128)S(1)}, u32[]{:S(2)}, u32[]{:S(2)}) %collective-permute-start.1) | collective-permute-done | bytes 524320 | tf_op jit(solution)/shard_map/ppermute | solution.py:174
  30.3 1.2 collective-permute-start.2
  31.5 1.7 %collective-permute-done.2 = f32[8,128,128]{2,1,0:T(8,128)} collective-permute-done((f32[8,128,128]{2,1,0:T(8,128)S(1)}, f32[8,128,128]{2,1,0:T(8,128)}, u32[]{:S(2)}, u32[]{:S(2)}) %collective-permute-start.2) | collective-permute-done | bytes 524320 | tf_op jit(solution)/shard_map/ppermute | solution.py:174
  33.2 1.1 broadcast_select_fusion.1
  34.4 0.8 copy-done
  35.2 0.1 copy-done.2
  35.3 1.2 collective-permute-start.3
  36.5 6.2 %collective-permute-done.3 = f32[4,128,128]{2,1,0:T(8,128)S(1)} collective-permute-done((f32[4,128,128]{2,1,0:T(8,128)S(1)}, f32[4,128,128]{2,1,0:T(8,128)S(1)}, u32[]{:S(2)}, u32[]{:S(2)}) %collective-permute-start.3) | collective-permute-done | bytes 262176 | tf_op jit(solution)/shard_map/ppermute | solution.py:174
  42.8 1.2 collective-permute-start.4
  44.0 1.5 collective-permute-start.6
  45.5 3.9 %collective-permute-done.4 = f32[4,128,128]{2,1,0:T(8,128)S(1)} collective-permute-done((f32[4,128,128]{2,1,0:T(8,128)S(1)}, f32[4,128,128]{2,1,0:T(8,128)S(1)}, u32[]{:S(2)}, u32[]{:S(2)}) %collective-permute-start.4) | collective-permute-done | bytes 262176 | tf_op jit(solution)/shard_map/ppermute | solution.py:179
  49.4 2.1 %collective-permute-start.5 = (f32[4,128,128]{2,1,0:T(8,128)S(1)}, f32[4,128,128]{2,1,0:T(8,128)S(1)}, u32[]{:S(2)}, u32[]{:S(2)}) collective-permute-start(f32[4,128,128]{2,1,0:T(8,128)S(1)} %collective-permute-done.4), channel_id=1, source_target_pairs={{0,1},{1,0},{2,3},{3,2},{4,5},{5,4},{6,7},{7,6},{8,9},{9,8},{10,11... | collective-permute-start | bytes 786440 | tf_op jit(solution)/shard_map/ppermute | solution.py:179
  51.5 1.2 collective-permute-done.5
  52.7 0.8 fusion.13
  53.5 0.7 copy-done.14
  54.2 0.2 collective-permute-start.7
  54.4 7.4 %collective-permute-done.7 = f32[4,128,128]{2,1,0:T(8,128)} collective-permute-done((f32[4,128,128]{2,1,0:T(8,128)S(1)}, f32[4,128,128]{2,1,0:T(8,128)}, u32[]{:S(2)}, u32[]{:S(2)}) %collective-permute-start.7) | collective-permute-done | bytes 262176 | tf_op jit(solution)/shard_map/ppermute | solution.py:174
  61.8 1.2 collective-permute-start.8
  63.0 4.8 %copy.9 = f32[10,16,1024]{0,2,1:T(8,128)} copy(f32[10,16,1024]{2,1,0:T(8,128)S(1)} %copy-done.15) | data formatting | bytes 1310720 | tf_op args[3]
  67.8 7.5 %shard_map.59.l_ref = f32[1024,512]{1,0:T(8,128)} custom-call(bf16[1024,2048]{1,0:T(8,128)(2,1)} %q_ref.15, bf16[1024,2048]{1,0:T(8,128)(2,1)} %k_ref.9, bf16[1024,2048]{1,0:T(8,128)(2,1)} %v_ref.9, f32[16,1024,10]{2,1,0:T(8,128)} %bitcast.31, f32[3,256,256]{2,1,0:T(8,128)} %constant.27.clone.c_ref), custom_call_target="tpu_custom_call" | custom-call | flops 1342177280 | bytes 5242880 | tf_op jit(solution)/shard_map/pallas_call | solution.py:93
  75.3 1.5 collective-permute-start.10
  76.9 7.4 %shard_map.58.l_ref = f32[1024,512]{1,0:T(8,128)} custom-call(bf16[1024,2048]{1,0:T(8,128)(2,1)} %q_ref.15, bf16[1024,2048]{1,0:T(8,128)(2,1)} %k_ref.9, bf16[1024,2048]{1,0:T(8,128)(2,1)} %v_ref.9, f32[16,1024,10]{2,1,0:T(8,128)} %bitcast.32, f32[3,256,256]{2,1,0:T(8,128)} %constant.27.clone.c_ref), custom_call_target="tpu_custom_call" | custom-call | flops 1342177280 | bytes 5242880 | tf_op jit(solution)/shard_map/pallas_call | solution.py:93
  84.3 7.4 %shard_map.57.l_ref = f32[1024,512]{1,0:T(8,128)} custom-call(bf16[1024,2048]{1,0:T(8,128)(2,1)} %q_ref.15, bf16[1024,2048]{1,0:T(8,128)(2,1)} %k_ref.9, bf16[1024,2048]{1,0:T(8,128)(2,1)} %v_ref.9, f32[16,1024,10]{2,1,0:T(8,128)} %bitcast.33, f32[3,256,256]{2,1,0:T(8,128)} %constant.27.clone.c_ref), custom_call_target="tpu_custom_call" | custom-call | flops 1342177280 | bytes 5242880 | tf_op jit(solution)/shard_map/pallas_call | solution.py:93
  91.6 7.4 %shard_map.56.l_ref = f32[1024,512]{1,0:T(8,128)} custom-call(bf16[1024,2048]{1,0:T(8,128)(2,1)} %q_ref.15, bf16[1024,2048]{1,0:T(8,128)(2,1)} %k_ref.9, bf16[1024,2048]{1,0:T(8,128)(2,1)} %v_ref.9, f32[16,1024,10]{2,1,0:T(8,128)} %bitcast.34, f32[3,256,256]{2,1,0:T(8,128)} %constant.27.clone.c_ref), custom_call_target="tpu_custom_call" | custom-call | flops 1342177280 | bytes 5242880 | tf_op jit(solution)/shard_map/pallas_call | solution.py:93
  99.1 1.2 fusion.12
  100.3 1.4 collective-permute-start.11
  101.8 2.2 %fusion.5 = bf16[5,16,128,128]{3,2,1,0:T(8,128)(2,1)} fusion(f32[16,128,128]{2,1,0:T(8,128)} %copy-done.4, f32[]{:T(128)S(6)} %convert_element_type.58), kind=kLoop, calls=%fused_computation.12 | loop fusion | flops 524287 | bytes 1572868
  104.0 0.9 fusion.9
  104.9 12.1 %collective-permute-done.11 = f32[4,128,128]{2,1,0:T(8,128)S(1)} collective-permute-done((f32[4,128,128]{2,1,0:T(8,128)S(1)}, f32[4,128,128]{2,1,0:T(8,128)S(1)}, u32[]{:S(2)}, u32[]{:S(2)}) %collective-permute-start.11) | collective-permute-done | bytes 262176 | tf_op jit(solution)/shard_map/ppermute | solution.py:174
  117.0 0.3 collective-permute-start.12
  117.3 0.1 select_bitcast_fusion.11
  117.5 0.9 fusion.8
  118.4 0.8 collective-permute-start.14
  119.2 5.2 %collective-permute-done.12 = f32[4,128,128]{2,1,0:T(8,128)S(1)} collective-permute-done((f32[4,128,128]{2,1,0:T(8,128)S(1)}, f32[4,128,128]{2,1,0:T(8,128)S(1)}, u32[]{:S(2)}, u32[]{:S(2)}) %collective-permute-start.12) | collective-permute-done | bytes 262176 | tf_op jit(solution)/shard_map/ppermute | solution.py:179
  124.4 1.3 collective-permute-start.13
  125.7 1.3 select_bitcast_fusion.7
  127.0 0.9 fusion.7
  128.0 0.1 select_bitcast_fusion.3
  128.2 0.9 fusion.6.s_ref
  129.1 6.3 %shard_map.60.rest_0_ = f32[1024,2048]{1,0:T(8,128)} custom-call(bf16[1024,2048]{1,0:T(8,128)(2,1)} %q_ref.15, bf16[5,16,128,128]{3,2,1,0:T(8,128)(2,1)} %fusion.6.s_ref, f32[16,1024,10]{2,1,0:T(8,128)} %bitcast.35, f32[1024,512]{1,0:T(8,128)} %shard_map.59.l_ref), custom_call_target="tpu_custom_call" | custom-call | flops 671088640 | bytes 5242880 | tf_op jit(solution)/shard_map/pallas_call | solution.py:149
  135.4 6.3 %shard_map.61.rest_0_ = f32[1024,2048]{1,0:T(8,128)} custom-call(bf16[1024,2048]{1,0:T(8,128)(2,1)} %q_ref.15, bf16[5,16,128,128]{3,2,1,0:T(8,128)(2,1)} %fusion.6.s_ref, f32[16,1024,10]{2,1,0:T(8,128)} %bitcast.36, f32[1024,512]{1,0:T(8,128)} %shard_map.58.l_ref, f32[1024,2048]{1,0:T(8,128)} %shard_map.60.rest_0_), custom_call_target="tpu_custom_call", output_to_operand_aliasing={{}: (4, {})} | custom-call | flops 671088640 | bytes 5242880 | tf_op jit(solution)/shard_map/pallas_call | solution.py:149
  141.7 6.3 %shard_map.62.rest_0_ = f32[1024,2048]{1,0:T(8,128)} custom-call(bf16[1024,2048]{1,0:T(8,128)(2,1)} %q_ref.15, bf16[5,16,128,128]{3,2,1,0:T(8,128)(2,1)} %fusion.6.s_ref, f32[16,1024,10]{2,1,0:T(8,128)} %bitcast.37, f32[1024,512]{1,0:T(8,128)} %shard_map.57.l_ref, f32[1024,2048]{1,0:T(8,128)} %shard_map.61.rest_0_), custom_call_target="tpu_custom_call", output_to_operand_aliasing={{}: (4, {})} | custom-call | flops 671088640 | bytes 5242880 | tf_op jit(solution)/shard_map/pallas_call | solution.py:149
  148.0 6.3 %shard_map.63 = f32[1024,2048]{1,0:T(8,128)} custom-call(bf16[1024,2048]{1,0:T(8,128)(2,1)} %q_ref.15, bf16[5,16,128,128]{3,2,1,0:T(8,128)(2,1)} %fusion.6.s_ref, f32[16,1024,10]{2,1,0:T(8,128)} %bitcast.38, f32[1024,512]{1,0:T(8,128)} %shard_map.56.l_ref, f32[1024,2048]{1,0:T(8,128)} %shard_map.62.rest_0_), custom_call_target="tpu_custom_call", output_to_operand_aliasing={{}: (4, {})} | custom-call | flops 671088640 | bytes 5242880 | tf_op jit(solution)/shard_map/pallas_call | solution.py:149
  (39 shorter events, 0.3 us)
Async XLA Ops:
  12.2 3.2 %collective-permute-start = (f32[16,128,128]{2,1,0:T(8,128)}, f32[16,128,128]{2,1,0:T(8,128)S(1)}, u32[]{:S(2)}, u32[]{:S(2)}) collective-permute-start(f32[16,128,128]{2,1,0:T(8,128)} %shard_map.55), channel_id=1, source_target_pairs={{0,1},{1,0},{2,3},{3,2},{4,5},{5,4},{6,7},{7,6},{8,9},{9,8},{10,11... | collective-permute-start | bytes 3145736 | tf_op jit(solution)/shard_map/ppermute | solution.py:174
  15.3 19.0 %copy-start.4 = (f32[16,128,128]{2,1,0:T(8,128)}, f32[16,128,128]{2,1,0:T(8,128)S(1)}, u32[]{:S(2)}) copy-start(f32[16,128,128]{2,1,0:T(8,128)S(1)} %collective-permute-done) | copy-start | bytes 3145732
  17.1 13.2 %collective-permute-start.1 = (f32[8,128,128]{2,1,0:T(8,128)S(1)}, f32[8,128,128]{2,1,0:T(8,128)S(1)}, u32[]{:S(2)}, u32[]{:S(2)}) collective-permute-start(f32[8,128,128]{2,1,0:T(8,128)S(1)} %constant_dynamic-slice_fusion), channel_id=1, source_target_pairs={{0,2},{2,0},{1,3},{3,1},{4,6},{6,4},{5,7},{7,5},{8,10},{10,8},{9,1... | collective-permute-start | bytes 1572872 | tf_op jit(solution)/shard_map/ppermute | solution.py:174
  30.3 2.9 %collective-permute-start.2 = (f32[8,128,128]{2,1,0:T(8,128)S(1)}, f32[8,128,128]{2,1,0:T(8,128)}, u32[]{:S(2)}, u32[]{:S(2)}) collective-permute-start(f32[8,128,128]{2,1,0:T(8,128)S(1)} %collective-permute-done.1), channel_id=1, source_target_pairs={{0,1},{1,0},{2,3},{3,2},{4,5},{5,4},{6,7},{7,6},{8,9},{9,8},{10,11... | collective-permute-start | bytes 1572872 | tf_op jit(solution)/shard_map/ppermute | solution.py:174
  31.5 31.5 %copy-start.15 = (f32[10,16,1024]{2,1,0:T(8,128)S(1)}, f32[10,16,1024]{2,1,0:T(8,128)}, u32[]{:S(2)}) copy-start(f32[10,16,1024]{2,1,0:T(8,128)} %param.8) | copy-start | bytes 1966084
  34.3 0.8 copy-start
  34.3 1.0 copy-start.2
  35.3 7.5 %collective-permute-start.3 = (f32[4,128,128]{2,1,0:T(8,128)S(1)}, f32[4,128,128]{2,1,0:T(8,128)S(1)}, u32[]{:S(2)}, u32[]{:S(2)}) collective-permute-start(f32[4,128,128]{2,1,0:T(8,128)S(1)} %fusion.11), channel_id=1, source_target_pairs={{0,4},{4,0},{8,12},{12,8},{16,20},{20,16},{24,28},{28,24},{1,5},{5... | collective-permute-start | bytes 786440 | tf_op jit(solution)/shard_map/ppermute | solution.py:174
  42.8 25.0 %copy-start.5 = (f32[4,128,128]{2,1,0:T(8,128)}, f32[4,128,128]{2,1,0:T(8,128)S(1)}, u32[]{:S(2)}) copy-start(f32[4,128,128]{2,1,0:T(8,128)S(1)} %collective-permute-done.3) | copy-start | bytes 786436
  42.8 6.6 %collective-permute-start.4 = (f32[4,128,128]{2,1,0:T(8,128)S(1)}, f32[4,128,128]{2,1,0:T(8,128)S(1)}, u32[]{:S(2)}, u32[]{:S(2)}) collective-permute-start(f32[4,128,128]{2,1,0:T(8,128)S(1)} %collective-permute-done.3), channel_id=1, source_target_pairs={{0,2},{1,3},{2,0},{3,1},{4,6},{5,7},{6,4},{7,5},{8,10},{9,11},{10,... | collective-permute-start | bytes 786440 | tf_op jit(solution)/shard_map/ppermute | solution.py:179
  44.0 7.5 %collective-permute-start.6 = (f32[4,128,128]{2,1,0:T(8,128)S(1)}, f32[4,128,128]{2,1,0:T(8,128)S(1)}, u32[]{:S(2)}, u32[]{:S(2)}) collective-permute-start(f32[4,128,128]{2,1,0:T(8,128)S(1)} %collective-permute-done.3), channel_id=1, source_target_pairs={{0,1},{1,0},{2,3},{3,2},{4,5},{5,4},{6,7},{7,6},{8,9},{9,8},{10,11... | collective-permute-start | bytes 786440 | tf_op jit(solution)/shard_map/ppermute | solution.py:179
  49.4 18.4 %copy-start.7 = (f32[4,128,128]{2,1,0:T(8,128)}, f32[4,128,128]{2,1,0:T(8,128)S(1)}, u32[]{:S(2)}) copy-start(f32[4,128,128]{2,1,0:T(8,128)S(1)} %collective-permute-done.4) | copy-start | bytes 786436
  49.4 3.2 %collective-permute-start.5 = (f32[4,128,128]{2,1,0:T(8,128)S(1)}, f32[4,128,128]{2,1,0:T(8,128)S(1)}, u32[]{:S(2)}, u32[]{:S(2)}) collective-permute-start(f32[4,128,128]{2,1,0:T(8,128)S(1)} %collective-permute-done.4), channel_id=1, source_target_pairs={{0,1},{1,0},{2,3},{3,2},{4,5},{5,4},{6,7},{7,6},{8,9},{9,8},{10,11... | collective-permute-start | bytes 786440 | tf_op jit(solution)/shard_map/ppermute | solution.py:179
  51.5 16.3 %copy-start.9 = (f32[4,128,128]{2,1,0:T(8,128)}, f32[4,128,128]{2,1,0:T(8,128)S(1)}, u32[]{:S(2)}) copy-start(f32[4,128,128]{2,1,0:T(8,128)S(1)} %collective-permute-done.6) | copy-start | bytes 786436
  52.7 15.2 %copy-start.11 = (f32[4,128,128]{2,1,0:T(8,128)}, f32[4,128,128]{2,1,0:T(8,128)S(1)}, u32[]{:S(2)}) copy-start(f32[4,128,128]{2,1,0:T(8,128)S(1)} %collective-permute-done.5) | copy-start | bytes 786436
  53.5 0.7 copy-start.14
  54.2 7.6 %collective-permute-start.7 = (f32[4,128,128]{2,1,0:T(8,128)S(1)}, f32[4,128,128]{2,1,0:T(8,128)}, u32[]{:S(2)}, u32[]{:S(2)}) collective-permute-start(f32[4,128,128]{2,1,0:T(8,128)S(1)} %get-tuple-element.18), channel_id=1, source_target_pairs={{0,8},{8,0},{4,12},{12,4},{16,24},{24,16},{20,28},{28,20},{1,9},{9... | collective-permute-start | bytes 786440 | tf_op jit(solution)/shard_map/ppermute | solution.py:174
  61.8 15.0 %collective-permute-start.8 = (f32[4,128,128]{2,1,0:T(8,128)}, f32[4,128,128]{2,1,0:T(8,128)}, u32[]{:S(2)}, u32[]{:S(2)}) collective-permute-start(f32[4,128,128]{2,1,0:T(8,128)} %collective-permute-done.7), channel_id=1, source_target_pairs={{0,2},{1,3},{2,0},{3,1},{4,6},{5,7},{6,4},{7,5},{8,10},{9,11},{10,... | collective-permute-start | bytes 786440 | tf_op jit(solution)/shard_map/ppermute | solution.py:179
  75.3 23.8 %collective-permute-start.10 = (f32[4,128,128]{2,1,0:T(8,128)}, f32[4,128,128]{2,1,0:T(8,128)}, u32[]{:S(2)}, u32[]{:S(2)}) collective-permute-start(f32[4,128,128]{2,1,0:T(8,128)} %collective-permute-done.7), channel_id=1, source_target_pairs={{0,1},{1,0},{2,3},{3,2},{4,5},{5,4},{6,7},{7,6},{8,9},{9,8},{10,11... | collective-permute-start | bytes 786440 | tf_op jit(solution)/shard_map/ppermute | solution.py:179
  76.8 22.3 %collective-permute-start.9 = (f32[4,128,128]{2,1,0:T(8,128)}, f32[4,128,128]{2,1,0:T(8,128)}, u32[]{:S(2)}, u32[]{:S(2)}) collective-permute-start(f32[4,128,128]{2,1,0:T(8,128)} %collective-permute-done.8), channel_id=1, source_target_pairs={{0,1},{1,0},{2,3},{3,2},{4,5},{5,4},{6,7},{7,6},{8,9},{9,8},{10,11... | collective-permute-start | bytes 786440 | tf_op jit(solution)/shard_map/ppermute | solution.py:179
  99.0 4.9 %copy-start.1 = (f32[8,128,128]{2,1,0:T(8,128)S(1)}, f32[8,128,128]{2,1,0:T(8,128)}, u32[]{:S(2)}) copy-start(f32[8,128,128]{2,1,0:T(8,128)} %copy-done) | copy-start | bytes 1572868
  99.0 4.9 %copy-start.3 = (f32[8,128,128]{2,1,0:T(8,128)S(1)}, f32[8,128,128]{2,1,0:T(8,128)}, u32[]{:S(2)}) copy-start(f32[8,128,128]{2,1,0:T(8,128)} %copy-done.2) | copy-start | bytes 1572868
  99.0 18.3 %copy-start.6 = (f32[4,128,128]{2,1,0:T(8,128)S(1)}, f32[4,128,128]{2,1,0:T(8,128)}, u32[]{:S(2)}) copy-start(f32[4,128,128]{2,1,0:T(8,128)} %copy-done.5) | copy-start | bytes 786436
  99.0 18.3 %copy-start.8 = (f32[4,128,128]{2,1,0:T(8,128)S(1)}, f32[4,128,128]{2,1,0:T(8,128)}, u32[]{:S(2)}) copy-start(f32[4,128,128]{2,1,0:T(8,128)} %copy-done.7) | copy-start | bytes 786436
  99.0 18.3 %copy-start.10 = (f32[4,128,128]{2,1,0:T(8,128)S(1)}, f32[4,128,128]{2,1,0:T(8,128)}, u32[]{:S(2)}) copy-start(f32[4,128,128]{2,1,0:T(8,128)} %copy-done.9) | copy-start | bytes 786436
  99.0 18.3 %copy-start.12 = (f32[4,128,128]{2,1,0:T(8,128)S(1)}, f32[4,128,128]{2,1,0:T(8,128)}, u32[]{:S(2)}) copy-start(f32[4,128,128]{2,1,0:T(8,128)} %copy-done.11) | copy-start | bytes 786436
  100.3 17.2 %copy-start.13 = (f32[1,4,128,128]{3,2,1,0:T(8,128)S(1)}, f32[1,4,128,128]{3,2,1,0:T(8,128)}, u32[]{:S(2)}) copy-start(f32[1,4,128,128]{3,2,1,0:T(8,128)} %get-tuple-element.19) | copy-start | bytes 786436
  100.3 16.7 %collective-permute-start.11 = (f32[4,128,128]{2,1,0:T(8,128)S(1)}, f32[4,128,128]{2,1,0:T(8,128)S(1)}, u32[]{:S(2)}, u32[]{:S(2)}) collective-permute-start(f32[4,128,128]{2,1,0:T(8,128)S(1)} %get-tuple-element.16), channel_id=1, source_target_pairs={{0,16},{4,20},{8,24},{12,28},{1,17},{5,21},{9,25},{13,29},{2,18},{... | collective-permute-start | bytes 786440 | tf_op jit(solution)/shard_map/ppermute | solution.py:174
  117.0 7.4 %collective-permute-start.12 = (f32[4,128,128]{2,1,0:T(8,128)S(1)}, f32[4,128,128]{2,1,0:T(8,128)S(1)}, u32[]{:S(2)}, u32[]{:S(2)}) collective-permute-start(f32[4,128,128]{2,1,0:T(8,128)S(1)} %collective-permute-done.11), channel_id=1, source_target_pairs={{0,2},{1,3},{2,0},{3,1},{4,6},{5,7},{6,4},{7,5},{8,10},{9,11},{10,... | collective-permute-start | bytes 786440 | tf_op jit(solution)/shard_map/ppermute | solution.py:179
  118.4 9.6 %collective-permute-start.14 = (f32[4,128,128]{2,1,0:T(8,128)S(1)}, f32[4,128,128]{2,1,0:T(8,128)S(1)}, u32[]{:S(2)}, u32[]{:S(2)}) collective-permute-start(f32[4,128,128]{2,1,0:T(8,128)S(1)} %collective-permute-done.11), channel_id=1, source_target_pairs={{0,1},{1,0},{2,3},{3,2},{4,5},{5,4},{6,7},{7,6},{8,9},{9,8},{10,11... | collective-permute-start | bytes 786440 | tf_op jit(solution)/shard_map/ppermute | solution.py:179
  124.4 3.6 %collective-permute-start.13 = (f32[4,128,128]{2,1,0:T(8,128)S(1)}, f32[4,128,128]{2,1,0:T(8,128)S(1)}, u32[]{:S(2)}, u32[]{:S(2)}) collective-permute-start(f32[4,128,128]{2,1,0:T(8,128)S(1)} %collective-permute-done.12), channel_id=1, source_target_pairs={{0,1},{1,0},{2,3},{3,2},{4,5},{5,4},{6,7},{7,6},{8,9},{9,8},{10,11... | collective-permute-start | bytes 786440 | tf_op jit(solution)/shard_map/ppermute | solution.py:179
